TPU v7x, 32 devices: a whole 2x2x4 slice. The times are simulated.
32 devices in a mesh: dp: 4 (over x, core), pipe: 2 (over y), tensor: 4 (over z).
Axes of the slice: x: 2, y: 2, z: 4, core: 2. Of those that a mesh axis runs over, the one named last changes fastest.
Arguments:
- layer_input: bfloat16 [4, 2, 512, 8192], P('dp', 'pipe', None, 'tensor'), may hold values from -40 to 40
- output_grad: bfloat16 [4, 2, 512, 8192], P('dp', 'pipe', None, 'tensor'), may hold values from -6 to 6
- kv_grad: bfloat16 [4, 2, 512, 2048], P('dp', 'pipe', None, 'tensor'), may hold values from -6 to 6
- norm_gain: bfloat16 [2, 8192], P('pipe', 'tensor'), may hold values from 0.5 to 1.5
- kv_weight: bfloat16 [2, 8192, 2048], P('pipe', 'tensor'), may hold values from -0.0625 to 0.0625
Outputs:
- upstream_grad: bfloat16 [4, 2, 512, 8192], P('dp', 'pipe', None, 'tensor')
- kv_weight_grad: bfloat16 [2, 8192, 2048], P('pipe', 'tensor', 'dp')
- gain_grad: float32 [2, 8192], P('pipe', 'tensor')
All inputs are finite; a program needn't handle non-finite values.
Results may differ from a plain program's by a relative error of at most 0.009.
Values may be sent and summed in bfloat16 or wider, within the bound.
No kernel may reach another device: no remote copies, remote signals or barrier semaphores. Data moves between devices by JAX's collectives and lax.ppermute only.
A program may use at most 128 MiB of HBM per device.

v0:
```python
import jax
import jax.numpy as jnp
from jax import lax
from jax.sharding import PartitionSpec as P

D = 8192


def from_behind(block, axis, distance):
    devices = range(lax.axis_size(axis))
    route = [(i - distance, i) for i in devices if i - distance in devices]
    return lax.ppermute(block, axis, route)


def on_device(layer_input, output_grad, kv_grad, norm_gain, kv_weight):
    rows = layer_input[0, 0]
    grad_out = output_grad[0, 0]
    grad_kv = kv_grad[0, 0]
    gain_f = norm_gain[0].astype(jnp.float32)
    weight = kv_weight[0]
    values = rows.astype(jnp.float32)
    local_squares = jnp.sum(values * values, axis=1, keepdims=True)
    total_squares = lax.psum(local_squares, "tensor")
    rstd = lax.rsqrt(total_squares / D + 1e-05)
    normed = values * rstd
    hidden = (normed * gain_f).astype(jnp.bfloat16)
    piece = lax.all_gather(grad_kv, "tensor", axis=1, tiled=True)
    row_total = lax.dot_general(
        piece, weight, (((1,), (1,)), ((), ())), preferred_element_type=jnp.float32
    )
    term = lax.dot_general(
        hidden, piece, (((0,), (0,)), ((), ())), preferred_element_type=jnp.float32
    )
    weight_total = term
    wgrad = weight_total
    scaled = gain_f * row_total
    local_dot = jnp.sum(scaled * normed, axis=1, keepdims=True)
    mean_term = lax.psum(local_dot, "tensor") / D
    input_grad = (grad_out.astype(jnp.float32) + rstd * (scaled - normed * mean_term)).astype(
        jnp.bfloat16
    )
    upstream = from_behind(input_grad, "pipe", -1)
    gain_part = jnp.sum(row_total * normed, axis=0)
    gain_total = lax.psum(gain_part, "dp")
    weight_total = lax.psum_scatter(
        wgrad.astype(jnp.bfloat16), "dp", scatter_dimension=1, tiled=True
    )
    return (upstream[None, None], weight_total[None], gain_total[None])


def solution(mesh):
    in_specs = (
        P("dp", "pipe", None, "tensor"),
        P("dp", "pipe", None, "tensor"),
        P("dp", "pipe", None, "tensor"),
        P("pipe", "tensor"),
        P("pipe", "tensor", None),
    )
    out_specs = (P("dp", "pipe", None, "tensor"), P("pipe", "tensor", "dp"), P("pipe", "tensor"))
    return jax.shard_map(
        on_device, mesh=mesh, in_specs=in_specs, out_specs=out_specs, check_vma=False
    )
```

profile of v0, /device:TPU:0, one launch (start us, length us, event | category | flops | bytes accessed | tf_op | source)
XLA Modules:
  0.0 152.9 jit_solution(5806783644709270451)
XLA Ops:
  7.2 0.0 all-gather.3.cloned.1.call-start
  7.2 0.7 all-gather.3.cloned.1.call-update
  7.9 0.0 reduce-scatter.2.cloned.1.call-start
  7.9 0.7 mul.69
  8.7 2.1 %fusion.13 = f32[512]{0:T(512)S(1)} fusion(bf16[1,1,512,2048]{3,2,1,0:T(8,128)(2,1)} %param.5), kind=kLoop, calls=%fused_computation.16 | loop fusion | flops 3145216 | bytes 2099200 | tf_op jit(solution)/shard_map/reduce_sum | solution.py:22
  10.7 13.7 %psum.21 = f32[512,1]{0,1:T(1,128)S(1)} all-reduce(f32[512,1]{0,1:T(1,128)S(1)} %bitcast.37), channel_id=1, replica_groups=mesh['dp'=4,'pipe'=2,'tensor'=4] {'tensor'}, use_global_device_ids=true, to_apply=%region_1.0 | all-reduce | flops 512 | bytes 4096 | tf_op jit(solution)/shard_map/psum | solution.py:23
  24.4 33.9 %all-gather.3.cloned.1.call-done = bf16[1,1,512,2048]{3,2,1,0:T(8,128)(2,1)} async-done(((bf16[1,1,512,512]{3,2,1,0:T(8,128)(2,1)}), bf16[1,1,512,2048]{3,2,1,0:T(8,128)(2,1)}) %all-gather.3.cloned.1.call-update) | async-done | bytes 2097168 | tf_op jit(solution)/shard_map/all_gather | solution.py:27
  58.3 10.1 %convolution_convert_fusion = bf16[2048,2048]{1,0:T(8,128)(2,1)} fusion(bf16[1,1,512,2048]{3,2,1,0:T(8,128)(2,1)} %param.5, bf16[1,1,512,2048]{3,2,1,0:T(8,128)(2,1)} %all-gather.3.cloned.1.call-done, f32[2048]{0:T(1024)S(1)} %bitcast.34, f32[512]{0:T(512)S(1)} %bitcast.39), kind=kOutput, calls=%fused_computation.2 | convolution fusion | flops 4303355904 | bytes 12593152 | tf_op jit(solution)/shard_map/dot_general | solution.py:31
  68.4 0.0 copy-start
  68.4 0.0 reduce-scatter.2.cloned.1.call-update
  68.4 1.6 %copy-done = bf16[1,1,512,2048]{3,2,1,0:T(8,128)(2,1)S(1)} copy-done((bf16[1,1,512,2048]{3,2,1,0:T(8,128)(2,1)S(1)}, bf16[1,1,512,2048]{3,2,1,0:T(8,128)(2,1)}, u32[]{:S(2)}) %copy-start) | copy-done | bytes 2097176
  70.0 11.8 %fusion.12 = (f32[2048]{0:T(1024)S(1)}, f32[512]{0:T(512)S(1)}, f32[512,2048]{1,0:T(8,128)}) fusion(bf16[1,1,512,2048]{3,2,1,0:T(8,128)(2,1)S(1)} %copy-done, f32[512]{0:T(512)S(1)} %bitcast.40, f32[2048]{0:T(1024)S(1)} %bitcast.35, bf16[1,2048,2048]{2,1,0:T(8,128)(2,1)} %param.9, bf16[1,1,512,2048]{3,2,1,0:T(8,128)(2,1)} %all-gather.3.cloned.1.call-done), kind=kOutput, calls=%fused_computation.15 | convolution fusion | flops 4302304768 | bytes 16797696 | tf_op jit(solution)/shard_map/dot_general | solution.py:28
  81.8 9.0 %psum.22 = f32[512,1]{0,1:T(1,128)S(1)} all-reduce(f32[512,1]{0,1:T(1,128)S(1)} %bitcast.43), channel_id=1, replica_groups=mesh['dp'=4,'pipe'=2,'tensor'=4] {'tensor'}, use_global_device_ids=true, to_apply=%region_3.0 | all-reduce | flops 512 | bytes 4096 | tf_op jit(solution)/shard_map/psum | solution.py:38
  90.8 5.7 %fusion.10 = bf16[512,2048]{1,0:T(8,128)(2,1)} fusion(f32[512,2048]{1,0:T(8,128)} %get-tuple-element.5, bf16[1,1,512,2048]{3,2,1,0:T(8,128)(2,1)} %param.6, bf16[1,1,512,2048]{3,2,1,0:T(8,128)(2,1)S(1)} %copy-done, f32[512]{0:T(512)S(1)} %bitcast.42, f32[2048]{0:T(1024)S(1)} %bitcast.36, f32[512]{0:T(512)S(1)} %bitcast.41), kind=kLoop, calls=%fused_computation.13 | loop fusion | flops 9437184 | bytes 10498048 | tf_op jit(solution)/shard_map/convert_element_type | solution.py:39
  96.5 1.3 collective-permute-start
  97.8 7.0 %psum.23 = f32[1,2048]{1,0:T(1,128)} all-reduce(f32[1,2048]{1,0:T(1,128)S(1)} %bitcast.38), channel_id=1, replica_groups=mesh['dp'=4,'pipe'=2,'tensor'=4] {'dp'}, use_global_device_ids=true, to_apply=%region_6.0 | all-reduce | flops 2048 | bytes 16384 | tf_op jit(solution)/shard_map/psum | solution.py:44
  104.8 39.9 %collective-permute-done = bf16[512,2048]{1,0:T(8,128)(2,1)S(1)} collective-permute-done((bf16[512,2048]{1,0:T(8,128)(2,1)}, bf16[512,2048]{1,0:T(8,128)(2,1)S(1)}, u32[]{:S(2)}, u32[]{:S(2)}) %collective-permute-start) | collective-permute-done | bytes 2097184 | tf_op jit(solution)/shard_map/ppermute | solution.py:12
  144.7 0.0 reduce-scatter.2.cloned.1.call-done
  144.7 1.3 copy.9
  (2 shorter events, 0.0 us)
Async XLA Ops:
  7.2 51.1 %all-gather.3.cloned.1.call-start = ((), (), s32[]{:S(2)}) async-start(), calls=%async_computation.2 | async-start | bytes 2621440 | tf_op jit(solution)/shard_map/all_gather | solution.py:27
  7.9 136.8 %reduce-scatter.2.cloned.1.call-start = ((), (), s32[]{:S(2)}) async-start(), calls=%async_computation.1 | async-start | bytes 10485760 | tf_op jit(solution)/shard_map/reduce_scatter | solution.py:45
  68.4 1.6 %copy-start = (bf16[1,1,512,2048]{3,2,1,0:T(8,128)(2,1)S(1)}, bf16[1,1,512,2048]{3,2,1,0:T(8,128)(2,1)}, u32[]{:S(2)}) copy-start(bf16[1,1,512,2048]{3,2,1,0:T(8,128)(2,1)} %param.5) | copy-start | bytes 6291460
  96.5 48.2 %collective-permute-start = (bf16[512,2048]{1,0:T(8,128)(2,1)}, bf16[512,2048]{1,0:T(8,128)(2,1)S(1)}, u32[]{:S(2)}, u32[]{:S(2)}) collective-permute-start(bf16[512,2048]{1,0:T(8,128)(2,1)} %fusion.10), channel_id=1, source_target_pairs={{4,0},{5,1},{6,2},{7,3},{12,8},{13,9},{14,10},{15,11},{20,16},{21,... | collective-permute-start | bytes 6291464 | tf_op jit(solution)/shard_map/ppermute | solution.py:12
Sparse Core Ops, SparseCore 0:
  9.6 48.6 all-gather.2
  68.5 70.6 reduce-scatter.1
where the time goes:
time: 153 us
  waiting for transfers between devices  74.5 us (49%)
  blocking collectives  29.6 us (19%)
  matrix products  21.9 us (14%)
  between operations  14.1 us (9%)
  other arithmetic  8.53 us (6%)
  local copies, waits for them, and re-layouts  2.89 us (2%)
    ppermute x1, waiting for transfers between devices, from_behind(): return lax.ppermute(block, axis, route)  39.9 us
    all_gather x1, waiting for transfers between devices, on_device(): piece = lax.all_gather(grad_kv, 'tensor', axis=1, tiled=True)  33.9 us
    psum x1, blocking collectives, on_device(): total_squares = lax.psum(local_squares, 'tensor')  13.7 us
    dot_general x1, matrix products, on_device(): lax.dot_general(piece, weight, (((1,), (1,)), ((), ())), preferred_elemen...  11.8 us
    dot_general x1, matrix products, on_device(): lax.dot_general(hidden, piece, (((0,), (0,)), ((), ())), preferred_elemen...  10.1 us
    psum x1, blocking collectives, on_device(): mean_term = lax.psum(local_dot, 'tensor') / D  8.96 us
    psum x1, blocking collectives, on_device(): gain_total = lax.psum(gain_part, 'dp')  7.03 us
    convert_element_type x1, other arithmetic, on_device(): (grad_out.astype(jnp.float32) + rstd * (scaled - normed * mean_term)).ast...  5.73 us
  transfers between devices with their start and end apart: 3, of which 2 were waited for; matrix products, arithmetic and copies ran while one was open for 13% of the time, Pallas kernels for 0%

commit v1 on v0

--- a/solution.py
+++ b/solution.py
@@ -24,7 +24,26 @@
     rstd = lax.rsqrt(total_squares / D + 1e-05)
     normed = values * rstd
     hidden = (normed * gain_f).astype(jnp.bfloat16)
-    piece = lax.all_gather(grad_kv, "tensor", axis=1, tiled=True)
+    devices_2, index, rows_2 = (lax.axis_size("tensor"), lax.axis_index("tensor"), grad_kv.shape[1])
+    right = [(i_2, (i_2 + 1) % devices_2) for i_2 in range(devices_2)]
+    left = [(i_2, (i_2 - 1) % devices_2) for i_2 in range(devices_2)]
+    out = jnp.zeros(
+        (*grad_kv.shape[:1], devices_2 * rows_2, *grad_kv.shape[1 + 1 :]), grad_kv.dtype
+    )
+    out = lax.dynamic_update_slice_in_dim(out, grad_kv, index * rows_2, axis=1)
+    from_left = from_right = grad_kv
+    half = devices_2 // 2
+    for step in range(1, half + 1):
+        from_left = lax.ppermute(from_left, "tensor", right)
+        out = lax.dynamic_update_slice_in_dim(
+            out, from_left, (index - step) % devices_2 * rows_2, axis=1
+        )
+        if step < devices_2 - half:
+            from_right = lax.ppermute(from_right, "tensor", left)
+            out = lax.dynamic_update_slice_in_dim(
+                out, from_right, (index + step) % devices_2 * rows_2, axis=1
+            )
+    piece = out
     row_total = lax.dot_general(
         piece, weight, (((1,), (1,)), ((), ())), preferred_element_type=jnp.float32
     )

time: 153 us -> 141 us (0.922)
  waiting for transfers between devices: 74.5 us -> 47.1 us
  blocking collectives: 29.6 us -> 40.1 us
  starting transfers between devices: 1.36 us -> 6.81 us
  matrix products: 21.9 us -> 18.4 us
  local copies, waits for them, and re-layouts: 2.89 us -> 5.2 us
    all_gather x1 -> x0, waiting for transfers between devices: 33.9 us -> none  [on_device(): piece = lax.all_gather(grad_kv, 'tensor', axis=1, tiled=True)]
    ppermute x0 -> x3, waiting for transfers between devices: none -> 11.2 us  [the longest x2 11.2 us: on_device(): from_left = lax.ppermute(from_left, 'tensor', right)]
    psum x1, blocking collectives: 13.7 us -> 24.7 us  [on_device(): total_squares = lax.psum(local_squares, 'tensor')]
    ppermute x0 -> x3, starting transfers between devices: none -> 5.49 us  [the longest x2 3.4 us: on_device(): from_left = lax.ppermute(from_left, 'tensor', right)]
    ppermute x1, waiting for transfers between devices: 39.9 us -> 35.7 us  [from_behind(): return lax.ppermute(block, axis, route)]
    dot_general x1, matrix products: 10.1 us -> 6.93 us  [on_device(): lax.dot_general(hidden, piece, (((0,), (0,)), ((), ())), preferred_elemen...]
    dynamic_update_slice x0 -> x4, local copies, waits for them, and re-layouts: none -> 2.32 us  [the longest x2 1.16 us: on_device(): lax.dynamic_update_slice_in_dim(out, from_left, (index - step) % devices_...]
  transfers between devices with their start and end apart: 3 -> 5, of which waited for: 2 -> 3; matrix products, arithmetic and copies ran while one was open for 13% -> 16% of each run, Pallas kernels for 0% -> 0%
where the time goes in v1:
time: 141 us
  waiting for transfers between devices  47.1 us (33%)
  blocking collectives  40.1 us (28%)
  matrix products  18.4 us (13%)
  between operations  14.2 us (10%)
  other arithmetic  9.06 us (6%)
  starting transfers between devices  6.81 us (5%)
  local copies, waits for them, and re-layouts  5.2 us (4%)
    ppermute x1, waiting for transfers between devices, from_behind(): return lax.ppermute(block, axis, route)  35.7 us
    psum x1, blocking collectives, on_device(): total_squares = lax.psum(local_squares, 'tensor')  24.7 us
    dot_general x1, matrix products, on_device(): lax.dot_general(piece, weight, (((1,), (1,)), ((), ())), preferred_elemen...  11.5 us
    ppermute x2, waiting for transfers between devices, on_device(): from_left = lax.ppermute(from_left, 'tensor', right)  11.2 us
    psum x1, blocking collectives, on_device(): mean_term = lax.psum(local_dot, 'tensor') / D  8.34 us
    psum x1, blocking collectives, on_device(): gain_total = lax.psum(gain_part, 'dp')  7.03 us
    dot_general x1, matrix products, on_device(): lax.dot_general(hidden, piece, (((0,), (0,)), ((), ())), preferred_elemen...  6.93 us
    convert_element_type x1, other arithmetic, on_device(): (grad_out.astype(jnp.float32) + rstd * (scaled - normed * mean_term)).ast...  6.26 us
  transfers between devices with their start and end apart: 5, of which 3 were waited for; matrix products, arithmetic and copies ran while one was open for 16% of the time, Pallas kernels for 0%

profile of v1, /device:TPU:0, one launch (start us, length us, event | category | flops | bytes accessed | tf_op | source)
XLA Modules:
  0.0 140.9 jit_solution(1324864764677390761)
XLA Ops:
  7.2 0.0 copy-start.2
  7.2 0.0 reduce-scatter.2.cloned.1.call-start
  7.2 0.0 copy-start
  7.2 3.1 %collective-permute-start = (bf16[512,512]{1,0:T(8,128)(2,1)}, bf16[512,512]{1,0:T(8,128)(2,1)S(1)}, u32[]{:S(2)}, u32[]{:S(2)}) collective-permute-start(bf16[512,512]{1,0:T(8,128)(2,1)} %bitcast.31), channel_id=1, source_target_pairs={{0,1},{1,2},{2,3},{3,0},{4,5},{5,6},{6,7},{7,4},{8,9},{9,10},{10,1... | collective-permute-start | bytes 1572872 | tf_op jit(solution)/shard_map/ppermute | solution.py:37
  10.3 2.1 %collective-permute-start.1 = (bf16[512,512]{1,0:T(8,128)(2,1)}, bf16[512,512]{1,0:T(8,128)(2,1)}, u32[]{:S(2)}, u32[]{:S(2)}) collective-permute-start(bf16[512,512]{1,0:T(8,128)(2,1)} %bitcast.32), channel_id=1, source_target_pairs={{0,3},{1,0},{2,1},{3,2},{4,7},{5,4},{6,5},{7,6},{8,11},{9,8},{10,9... | collective-permute-start | bytes 1572872 | tf_op jit(solution)/shard_map/ppermute | solution.py:42
  12.4 2.1 %fusion.13 = f32[512]{0:T(512)S(1)} fusion(bf16[1,1,512,2048]{3,2,1,0:T(8,128)(2,1)} %param.5), kind=kLoop, calls=%fused_computation.16 | loop fusion | flops 3145216 | bytes 2099200 | tf_op jit(solution)/shard_map/reduce_sum | solution.py:22
  14.5 24.7 %psum.21 = f32[512,1]{0,1:T(1,128)S(1)} all-reduce(f32[512,1]{0,1:T(1,128)S(1)} %bitcast.36), channel_id=1, replica_groups=mesh['dp'=4,'pipe'=2,'tensor'=4] {'tensor'}, use_global_device_ids=true, to_apply=%region_1.0 | all-reduce | flops 512 | bytes 4096 | tf_op jit(solution)/shard_map/psum | solution.py:23
  39.2 0.0 collective-permute-done
  39.2 0.3 collective-permute-start.2
  39.6 0.7 mul.85
  40.3 0.2 broadcast_in_dim.21
  40.6 0.0 copy-done.2
  40.6 0.1 constant_dynamic-update-slice_fusion.3
  40.7 0.1 constant_dynamic-update-slice_fusion.2
  40.7 0.0 collective-permute-done.1
  40.8 1.1 constant_dynamic-update-slice_fusion.1
  41.9 11.1 %collective-permute-done.2 = bf16[512,512]{1,0:T(8,128)(2,1)} collective-permute-done((bf16[512,512]{1,0:T(8,128)(2,1)S(1)}, bf16[512,512]{1,0:T(8,128)(2,1)}, u32[]{:S(2)}, u32[]{:S(2)}) %collective-permute-start.2) | collective-permute-done | bytes 524320 | tf_op jit(solution)/shard_map/ppermute | solution.py:37
  53.0 1.1 constant_dynamic-update-slice_fusion
  54.1 0.0 copy-start.1
  54.1 1.3 copy-done.1
  55.4 0.0 copy-done
  55.4 6.9 %convolution_convert_fusion = bf16[2048,2048]{1,0:T(8,128)(2,1)} fusion(bf16[512,2048]{1,0:T(8,128)(2,1)S(1)} %constant_dynamic-update-slice_fusion, bf16[1,1,512,2048]{3,2,1,0:T(8,128)(2,1)S(1)} %copy-done, f32[2048]{0:T(1024)S(1)} %bitcast.33, f32[512]{0:T(512)S(1)} %bitcast.38), kind=kOutput, calls=%fused_computation.2 | convolution fusion | flops 4303355904 | bytes 12593152 | tf_op jit(solution)/shard_map/dot_general | solution.py:50
  62.4 0.0 reduce-scatter.2.cloned.1.call-update
  62.4 11.5 %fusion.12 = (f32[2048]{0:T(1024)S(1)}, f32[512]{0:T(512)S(1)}, f32[512,2048]{1,0:T(8,128)}) fusion(bf16[1,1,512,2048]{3,2,1,0:T(8,128)(2,1)S(1)} %copy-done, f32[512]{0:T(512)S(1)} %bitcast.39, f32[2048]{0:T(1024)S(1)} %bitcast.34, bf16[512,2048]{1,0:T(8,128)(2,1)} %copy-done.1, bf16[1,2048,2048]{2,1,0:T(8,128)(2,1)} %param.9), kind=kOutput, calls=%fused_computation.15 | convolution fusion | flops 4302304768 | bytes 16797696 | tf_op jit(solution)/shard_map/dot_general | solution.py:47
  73.9 8.3 %psum.22 = f32[512,1]{0,1:T(1,128)S(1)} all-reduce(f32[512,1]{0,1:T(1,128)S(1)} %bitcast.42), channel_id=1, replica_groups=mesh['dp'=4,'pipe'=2,'tensor'=4] {'tensor'}, use_global_device_ids=true, to_apply=%region_3.4 | all-reduce | flops 512 | bytes 4096 | tf_op jit(solution)/shard_map/psum | solution.py:57
  82.3 6.3 %fusion.10 = bf16[512,2048]{1,0:T(8,128)(2,1)} fusion(f32[512,2048]{1,0:T(8,128)} %get-tuple-element.5, bf16[1,1,512,2048]{3,2,1,0:T(8,128)(2,1)} %param.6, bf16[1,1,512,2048]{3,2,1,0:T(8,128)(2,1)S(1)} %copy-done, f32[512]{0:T(512)S(1)} %bitcast.41, f32[2048]{0:T(1024)S(1)} %bitcast.35, f32[512]{0:T(512)S(1)} %bitcast.40), kind=kLoop, calls=%fused_computation.13 | loop fusion | flops 9437184 | bytes 10498048 | tf_op jit(solution)/shard_map/convert_element_type | solution.py:58
  88.5 1.3 collective-permute-start.3
  89.8 7.0 %psum.23 = f32[1,2048]{1,0:T(1,128)} all-reduce(f32[1,2048]{1,0:T(1,128)S(1)} %bitcast.37), channel_id=1, replica_groups=mesh['dp'=4,'pipe'=2,'tensor'=4] {'dp'}, use_global_device_ids=true, to_apply=%region_6.7 | all-reduce | flops 2048 | bytes 16384 | tf_op jit(solution)/shard_map/psum | solution.py:63
  96.8 35.7 %collective-permute-done.3 = bf16[512,2048]{1,0:T(8,128)(2,1)S(1)} collective-permute-done((bf16[512,2048]{1,0:T(8,128)(2,1)}, bf16[512,2048]{1,0:T(8,128)(2,1)S(1)}, u32[]{:S(2)}, u32[]{:S(2)}) %collective-permute-start.3) | collective-permute-done | bytes 2097184 | tf_op jit(solution)/shard_map/ppermute | solution.py:12
  132.6 0.2 reduce-scatter.2.cloned.1.call-done
  132.7 1.3 copy.13
  (2 shorter events, 0.0 us)
Async XLA Ops:
  7.2 33.4 %copy-start.2 = (bf16[1,1,512,512]{3,2,1,0:T(8,128)(2,1)S(1)}, bf16[1,1,512,512]{3,2,1,0:T(8,128)(2,1)}, u32[]{:S(2)}) copy-start(bf16[1,1,512,512]{3,2,1,0:T(8,128)(2,1)} %param.7) | copy-start | bytes 1572868
  7.2 125.6 %reduce-scatter.2.cloned.1.call-start = ((), (), s32[]{:S(2)}) async-start(), calls=%async_computation.1 | async-start | bytes 10485760 | tf_op jit(solution)/shard_map/reduce_scatter | solution.py:64
  7.2 48.2 %copy-start = (bf16[1,1,512,2048]{3,2,1,0:T(8,128)(2,1)S(1)}, bf16[1,1,512,2048]{3,2,1,0:T(8,128)(2,1)}, u32[]{:S(2)}) copy-start(bf16[1,1,512,2048]{3,2,1,0:T(8,128)(2,1)} %param.5) | copy-start | bytes 6291460
  7.2 32.0 %collective-permute-start = (bf16[512,512]{1,0:T(8,128)(2,1)}, bf16[512,512]{1,0:T(8,128)(2,1)S(1)}, u32[]{:S(2)}, u32[]{:S(2)}) collective-permute-start(bf16[512,512]{1,0:T(8,128)(2,1)} %bitcast.31), channel_id=1, source_target_pairs={{0,1},{1,2},{2,3},{3,0},{4,5},{5,6},{6,7},{7,4},{8,9},{9,10},{10,1... | collective-permute-start | bytes 1572872 | tf_op jit(solution)/shard_map/ppermute | solution.py:37
  10.3 30.4 %collective-permute-start.1 = (bf16[512,512]{1,0:T(8,128)(2,1)}, bf16[512,512]{1,0:T(8,128)(2,1)}, u32[]{:S(2)}, u32[]{:S(2)}) collective-permute-start(bf16[512,512]{1,0:T(8,128)(2,1)} %bitcast.32), channel_id=1, source_target_pairs={{0,3},{1,0},{2,1},{3,2},{4,7},{5,4},{6,5},{7,6},{8,11},{9,8},{10,9... | collective-permute-start | bytes 1572872 | tf_op jit(solution)/shard_map/ppermute | solution.py:42
  39.2 13.8 %collective-permute-start.2 = (bf16[512,512]{1,0:T(8,128)(2,1)S(1)}, bf16[512,512]{1,0:T(8,128)(2,1)}, u32[]{:S(2)}, u32[]{:S(2)}) collective-permute-start(bf16[512,512]{1,0:T(8,128)(2,1)S(1)} %collective-permute-done), channel_id=1, source_target_pairs={{0,1},{1,2},{2,3},{3,0},{4,5},{5,6},{6,7},{7,4},{8,9},{9,10},{10,1... | collective-permute-start | bytes 1572872 | tf_op jit(solution)/shard_map/ppermute | solution.py:37
  54.1 1.3 copy-start.1
  88.5 44.0 %collective-permute-start.3 = (bf16[512,2048]{1,0:T(8,128)(2,1)}, bf16[512,2048]{1,0:T(8,128)(2,1)S(1)}, u32[]{:S(2)}, u32[]{:S(2)}) collective-permute-start(bf16[512,2048]{1,0:T(8,128)(2,1)} %fusion.10), channel_id=1, source_target_pairs={{4,0},{5,1},{6,2},{7,3},{12,8},{13,9},{14,10},{15,11},{20,16},{21,... | collective-permute-start | bytes 6291464 | tf_op jit(solution)/shard_map/ppermute | solution.py:12
Sparse Core Ops, SparseCore 0:
  62.5 70.1 reduce-scatter.1
